TPU v7x, 32 devices: a whole 2x2x4 slice. The times are simulated.
32 devices in a mesh: segment: 4 (over z), ctx: 4 (over y, x), head: 2 (over core).
Axes of the slice: x: 2, y: 2, z: 4, core: 2. Of those that a mesh axis runs over, the one named last changes fastest.
Arguments:
- inputs: bfloat16 [4, 512, 5120], P('segment', 'ctx'), may hold values from -6 to 6
- query: bfloat16 [4, 512, 20, 128], P('segment', 'ctx', 'head'), may hold values from -32 to 32
- grad_out: bfloat16 [4, 512, 20, 128], P('segment', 'ctx', 'head'), may hold values from -6 to 6
- w_key: bfloat16 [4, 5120, 512], P('segment', None, 'head'), may hold values from -0.078125 to 0.078125
- w_value: bfloat16 [4, 5120, 512], P('segment', None, 'head'), may hold values from -0.078125 to 0.078125
- keep_mask: int32 [512], replicated, may hold values from 0 to 1
Outputs:
- grad_input: float32 [4, 512, 5120], P('segment', 'ctx', 'head')
All inputs are finite; a program needn't handle non-finite values.
Results may differ from a plain program's by a relative error of at most 0.022.
The roundings to bfloat16 on the way count: a program that leaves them out, or rounds other values in their place, can miss the bound.
Values may be sent and summed in bfloat16 or wider, within the bound.
No kernel may reach another device: no remote copies, remote signals or barrier semaphores. Data moves between devices by JAX's collectives and lax.ppermute only.
A program may use at most 192 MiB of HBM per device.

v0:
```python
import math
import jax
import jax.numpy as jnp
from jax import lax
from jax.sharding import PartitionSpec as P


def suffix_chain(own, axis):
    length, index = (lax.axis_size(axis), lax.axis_index(axis))
    total = own
    for k in range(length - 1):
        src_dev = length - 1 - k
        got = lax.ppermute(total.astype(jnp.bfloat16), axis, [(src_dev, src_dev - 1)])
        total = jnp.where(index == src_dev - 1, own + got.astype(jnp.float32), total)
    return total


def per_device(inputs, query, grad_out, w_key, w_value, keep_mask):
    tok_rows = inputs.shape[1]
    local_heads = query.shape[2]
    head_dim = query.shape[3]
    kv_cols = w_key.shape[2]
    kv_local = kv_cols // head_dim
    group_size = local_heads // kv_local
    scaling = 1.0 / math.sqrt(head_dim)
    tokens = inputs[0]
    key_rows = jnp.dot(tokens, w_key[0], preferred_element_type=jnp.float32).astype(jnp.bfloat16)
    value_rows = jnp.dot(tokens, w_value[0], preferred_element_type=jnp.float32).astype(
        jnp.bfloat16
    )
    kv_all = lax.all_gather(
        jnp.concatenate((key_rows, value_rows), axis=1), "ctx", axis=0, tiled=True
    )
    keys_all, values_all = (kv_all[:, : key_rows.shape[1]], kv_all[:, key_rows.shape[1] :])
    seq_rows = keys_all.shape[0]
    key_heads = keys_all.reshape(seq_rows, kv_local, head_dim)
    value_heads = values_all.reshape(seq_rows, kv_local, head_dim)
    query_heads = query[0].reshape(tok_rows, kv_local, group_size, head_dim)
    grad_heads = grad_out[0].reshape(tok_rows, kv_local, group_size, head_dim)
    query_major = jnp.moveaxis(query_heads, 1, 0)
    grad_major = jnp.moveaxis(grad_heads, 1, 0)
    ctx_index = lax.axis_index("ctx")
    first_row = ctx_index * tok_rows
    row_pos = first_row + jnp.arange(tok_rows, dtype=jnp.int32)[:, None]
    col_pos = jnp.arange(seq_rows, dtype=jnp.int32)[None, :]
    allowed = (col_pos <= row_pos) & ((keep_mask[None, :] == 1) | (col_pos == row_pos))

    def one_group(packed):
        query_group, grad_group, key_group, value_group = packed
        scores = (
            jnp.einsum("tgd,sd->gts", query_group, key_group, preferred_element_type=jnp.float32)
            * scaling
        )
        masked = jnp.where(allowed, scores, -1e30)
        top_score = jnp.max(masked, axis=-1, keepdims=True)
        totals = jnp.sum(
            jnp.where(allowed, jnp.exp(masked - top_score), 0.0), axis=-1, keepdims=True
        )
        log_total = top_score + jnp.log(totals)
        prob_full = jnp.where(allowed, jnp.exp(masked - log_total), 0.0)
        prob_low = prob_full.astype(jnp.bfloat16)
        attended = jnp.einsum(
            "gts,sd->tgd", prob_low, value_group, preferred_element_type=jnp.float32
        )
        row_dots = jnp.sum(grad_group.astype(jnp.float32) * attended, axis=-1)
        dprob = jnp.einsum(
            "tgd,sd->gts", grad_group, value_group, preferred_element_type=jnp.float32
        )
        score_low = (prob_full * (dprob - jnp.transpose(row_dots, (1, 0))[..., None])).astype(
            jnp.bfloat16
        )
        return (prob_low, score_low)

    probs_b, dscore_b = lax.map(
        one_group,
        (query_major, grad_major, jnp.moveaxis(key_heads, 1, 0), jnp.moveaxis(value_heads, 1, 0)),
    )

    def per_group(packed):
        prob_group, score_group, query_group, grad_group = packed
        value_term = jnp.einsum(
            "gts,tgd->sd", prob_group, grad_group, preferred_element_type=jnp.float32
        )
        key_term = (
            jnp.einsum("gts,tgd->sd", score_group, query_group, preferred_element_type=jnp.float32)
            * scaling
        )
        return (key_term, value_term)

    key_term, value_term = lax.map(per_group, (probs_b, dscore_b, query_major, grad_major))
    key_flat = jnp.moveaxis(key_term, 0, 1).reshape(tok_rows * lax.axis_size("ctx"), kv_cols)
    value_flat = jnp.moveaxis(value_term, 0, 1).reshape(tok_rows * lax.axis_size("ctx"), kv_cols)
    key_grads = lax.psum_scatter(
        jnp.concatenate((key_flat, value_flat), axis=1).astype(jnp.bfloat16),
        "ctx",
        scatter_dimension=0,
        tiled=True,
    ).astype(jnp.float32)
    grad_key = key_grads[:, :kv_cols].astype(jnp.bfloat16)
    grad_value = key_grads[:, kv_cols:].astype(jnp.bfloat16)
    contract = (((1,), (1,)), ((), ()))
    partial_sum = lax.dot_general(grad_key, w_key[0], contract, preferred_element_type=jnp.float32)
    partial_sum = partial_sum + lax.dot_general(
        grad_value, w_value[0], contract, preferred_element_type=jnp.float32
    )
    reduced = lax.psum_scatter(
        partial_sum.astype(jnp.bfloat16), "head", scatter_dimension=1, tiled=True
    ).astype(jnp.float32)
    result = suffix_chain(reduced, "segment")
    return result[None]


def solution(mesh):
    return jax.shard_map(
        per_device,
        mesh=mesh,
        in_specs=(
            P("segment", "ctx", None),
            P("segment", "ctx", "head", None),
            P("segment", "ctx", "head", None),
            P("segment", None, "head"),
            P("segment", None, "head"),
            P(),
        ),
        out_specs=P("segment", "ctx", "head"),
        check_vma=False,
    )
```

profile of v0, /device:TPU:0, one launch (start us, length us, event | category | flops | bytes accessed | tf_op | source)
XLA Modules:
  0.0 149.9 jit_solution(10421825341742242223)
XLA Ops:
  6.5 1.7 %copy-done = bf16[1,5120,256]{2,1,0:T(8,128)(2,1)S(1)} copy-done((bf16[1,5120,256]{2,1,0:T(8,128)(2,1)S(1)}, bf16[1,5120,256]{2,1,0:T(8,128)(2,1)}, u32[]{:S(2)}) %copy-start) | copy-done | bytes 2621464
  8.3 2.0 %fusion.56 = bf16[128,256]{1,0:T(8,128)(2,1)S(1)} fusion(bf16[1,5120,256]{2,1,0:T(8,128)(2,1)S(1)} %copy-done, bf16[1,128,5120]{2,1,0:T(8,128)(2,1)} %param.10), kind=kOutput, calls=%fused_computation.71 | convolution fusion | flops 335577088 | bytes 3997696 | tf_op jit(solution)/shard_map/dot_general | solution.py:27
  10.3 0.1 copy-done.1
  10.4 0.4 copy-done.4
  10.8 0.5 fusion.61
  11.3 11.7 %all_gather.3 = bf16[512,512]{1,0:T(8,128)(2,1)S(1)} all-gather(bf16[128,512]{1,0:T(8,128)(2,1)S(1)} %pad_maximum_fusion.1), channel_id=1, replica_groups=mesh['segment'=4,'ctx'=4,'head'=2] {'ctx'}, dimensions={0}, use_global_device_ids=true | all-gather | bytes 655360 | tf_op jit(solution)/shard_map/all_gather | solution.py:31
  23.0 0.8 slice_bitcast_fusion
  23.9 1.8 %bitcast_bitcast_fusion = (bf16[2,512,128]{2,1,0:T(8,128)(2,1)}, bf16[2,512,128]{2,1,0:T(8,128)(2,1)S(1)}) fusion(bf16[64,2,8,128]{3,2,1,0:T(8,128)(2,1)} %get-tuple-element.146, bf16[64,2,8,128]{3,2,1,0:T(8,128)(2,1)} %get-tuple-element.147), kind=kLoop, calls=%fused_computation.75 | loop fusion | bytes 1048576 | tf_op jit(solution)/shard_map/transpose | solution.py:76
  25.7 8.1 %while.26 = (s32[]{:T(128)}, bf16[2,5,128,512]{2,3,1,0:T(8,128)(2,1)}, bf16[2,5,128,512]{2,3,1,0:T(8,128)(2,1)}, bf16[2,512,128]{2,1,0:T(8,128)(2,1)S(1)}, bf16[...) while((s32[]{:T(128)}, ...), condition=%wide.region_4.5_spmd.clone, body=%wide.region_0.4_spmd.clone.sunk | while | flops 257735424 | bytes 10228865 | solution.py:74
  25.7 0.1 fusion.94
  25.9 0.4 fusion.95
  26.2 0.2 select_reduce_fusion.2
  26.5 0.3 copy-done.6
  26.8 0.6 fusion.96
  27.4 1.3 fusion.97
  28.7 1.1 bitcast_dynamic-update-slice_fusion.2
  29.8 0.1 fusion.94
  29.9 0.4 fusion.95
  30.3 0.2 select_reduce_fusion.2
  30.5 0.3 copy-done.6
  30.8 0.6 fusion.96
  31.4 1.3 fusion.97
  32.7 1.1 bitcast_dynamic-update-slice_fusion.2
  33.8 8.7 %while.25 = (s32[]{:T(128)}, bf16[2,512,128]{1,2,0:T(8,128)(2,1)}, bf16[2,512,128]{1,2,0:T(8,128)(2,1)}, bf16[2,5,128,512]{2,3,1,0:T(8,128)(2,1)}, bf16[2,128,5,...) while((s32[]{:T(128)}, bf16[2,512,128]{1,2,0:T(8,128)(2,1)}, ...), condition=%wide.region_6.7_spmd, body=%wide.region_5.6_spmd.sunk | while | flops 167903232 | bytes 2559061 | solution.py:90
  33.8 1.4 fusion.88
  35.2 0.1 copy.43
  35.4 0.7 constant_dynamic-update-slice_fusion.2
  36.0 2.1 %fusion.89 = bf16[2,512,128]{1,2,0:T(8,128)(2,1)} fusion(bf16[2,512,128]{1,2,0:T(8,128)(2,1)} %get-tuple-element.292, s32[]{:T(128)} %get-tuple-element.290, bf16[2,5,128,512]{2,3,1,0:T(8,128)(2,1)} %get-tuple-element.303, bf16[2,128,5,128]{3,1,2,0:T(8,128)(2,1)S(1)} %get-tuple-element.304), kind=kOutput, calls=%fused_computation.2.clone.1 | convolution fusion | flops 83886080 | bytes 1082880 | tf_op jit(solution)/shard_map/while/body/eval_jaxpr/gts,tgd->sd/dot_general | solution.py:81
  38.1 1.4 fusion.88
  39.6 0.1 copy.43
  39.7 0.7 constant_dynamic-update-slice_fusion.2
  40.4 2.1 %fusion.89 = bf16[2,512,128]{1,2,0:T(8,128)(2,1)} fusion(bf16[2,512,128]{1,2,0:T(8,128)(2,1)} %get-tuple-element.292, s32[]{:T(128)} %get-tuple-element.290, bf16[2,5,128,512]{2,3,1,0:T(8,128)(2,1)} %get-tuple-element.303, bf16[2,128,5,128]{3,1,2,0:T(8,128)(2,1)S(1)} %get-tuple-element.304), kind=kOutput, calls=%fused_computation.2.clone.1 | convolution fusion | flops 83886080 | bytes 1082880 | tf_op jit(solution)/shard_map/while/body/eval_jaxpr/gts,tgd->sd/dot_general | solution.py:81
  42.5 1.1 pad_maximum_fusion
  43.5 1.0 copy.30
  44.5 0.0 reduce-scatter.7.cloned.1.call-update
  44.6 0.0 reduce-scatter.5.cloned.1.call-start
  44.6 25.5 %reduce-scatter.7.cloned.1.call-done = bf16[128,512]{1,0:T(8,128)(2,1)} async-done(((bf16[512,512]{1,0:T(8,128)(2,1)}), bf16[128,512]{1,0:T(8,128)(2,1)}) %reduce-scatter.7.cloned.1.call-update) | async-done | bytes 131088
  70.1 2.0 %fusion.46 = f32[128,5120]{1,0:T(8,128)S(1)} fusion(bf16[1,5120,256]{2,1,0:T(8,128)(2,1)S(1)} %copy-done, bf16[128,512]{1,0:T(8,128)(2,1)} %reduce-scatter.7.cloned.1.call-done), kind=kOutput, calls=%fused_computation.57 | convolution fusion | flops 335544320 | bytes 5308416 | tf_op jit(solution)/shard_map/dot_general | solution.py:102
  72.1 2.1 %fusion.42 = bf16[128,5120]{1,0:T(8,128)(2,1)} fusion(f32[128,5120]{1,0:T(8,128)S(1)} %fusion.46, bf16[1,5120,256]{2,1,0:T(8,128)(2,1)S(1)} %copy-done.2, bf16[128,512]{1,0:T(8,128)(2,1)S(1)} %copy-done.7), kind=kOutput, calls=%fused_computation.53 | convolution fusion | flops 336855040 | bytes 6619136 | tf_op jit(solution)/shard_map/dot_general | solution.py:103
  74.1 0.0 reduce-scatter.5.cloned.1.call-update
  74.2 8.8 %reduce-scatter.5.cloned.1.call-done = bf16[128,2560]{1,0:T(8,128)(2,1)} async-done(((bf16[128,5120]{1,0:T(8,128)(2,1)}), bf16[128,2560]{1,0:T(8,128)(2,1)}) %reduce-scatter.5.cloned.1.call-update) | async-done | bytes 655376 | tf_op jit(solution)/shard_map/reduce_scatter | solution.py:106
  83.0 1.5 %collective-permute-start = (bf16[128,2560]{1,0:T(8,128)(2,1)}, bf16[128,2560]{1,0:T(8,128)(2,1)}, u32[]{:S(2)}, u32[]{:S(2)}) collective-permute-start(bf16[128,2560]{1,0:T(8,128)(2,1)} %reduce-scatter.5.cloned.1.call-done), channel_id=1, source_target_pairs={{24,16},{25,17},{26,18},{27,19},{28,20},{29,21},{30,22},{31,23}} | collective-permute-start | bytes 1966088 | tf_op jit(solution)/shard_map/ppermute | solution.py:13
  84.5 1.5 fusion.55
  85.9 1.5 %collective-permute-start.1 = (bf16[128,2560]{1,0:T(8,128)(2,1)S(1)}, bf16[128,2560]{1,0:T(8,128)(2,1)}, u32[]{:S(2)}, u32[]{:S(2)}) collective-permute-start(bf16[128,2560]{1,0:T(8,128)(2,1)S(1)} %fusion.55), channel_id=1, source_target_pairs={{16,8},{17,9},{18,10},{19,11},{20,12},{21,13},{22,14},{23,15}} | collective-permute-start | bytes 1966088 | tf_op jit(solution)/shard_map/ppermute | solution.py:13
  87.5 2.6 %fusion.66 = bf16[128,2560]{1,0:T(8,128)(2,1)} fusion(bf16[128,2560]{1,0:T(8,128)(2,1)} %collective-permute-done, bf16[128,2560]{1,0:T(8,128)(2,1)} %collective-permute-done.1, bf16[128,2560]{1,0:T(8,128)(2,1)} %reduce-scatter.5.cloned.1.call-done, pred[]{:T(512)S(6)} %eq.30, pred[]{:T(512)S(6)} %eq.29), kind=kLoop, calls=%fused_computation.73 | loop fusion | flops 2621440 | bytes 2621442 | tf_op jit(solution)/shard_map/convert_element_type | solution.py:13
  90.1 1.3 collective-permute-start.2
  91.4 48.7 %collective-permute-done.2 = bf16[128,2560]{1,0:T(8,128)(2,1)S(1)} collective-permute-done((bf16[128,2560]{1,0:T(8,128)(2,1)}, bf16[128,2560]{1,0:T(8,128)(2,1)S(1)}, u32[]{:S(2)}, u32[]{:S(2)}) %collective-permute-start.2) | collective-permute-done | bytes 655392 | tf_op jit(solution)/shard_map/ppermute | solution.py:13
  140.1 3.0 %fusion.52 = f32[1,128,2560]{2,1,0:T(8,128)} fusion(bf16[128,2560]{1,0:T(8,128)(2,1)} %reduce-scatter.5.cloned.1.call-done, bf16[128,2560]{1,0:T(8,128)(2,1)S(1)} %collective-permute-done.2, bf16[128,2560]{1,0:T(8,128)(2,1)} %collective-permute-done, bf16[128,2560]{1,0:T(8,128)(2,1)} %collective-permute-done.1, pred[]{:T(512)S(6)} %eq.30, pred[]{:T(512)S(6)} %eq.29, ...), kind=kLoop, calls=%fused_computation.67 | loop fusion | flops 3276800 | bytes 3932163 | tf_op jit(solution)/shard_map/broadcast_in_dim | solution.py:110
  (27 shorter events, 0.1 us)
Async XLA Ops:
  6.5 1.7 %copy-start = (bf16[1,5120,256]{2,1,0:T(8,128)(2,1)S(1)}, bf16[1,5120,256]{2,1,0:T(8,128)(2,1)}, u32[]{:S(2)}) copy-start(bf16[1,5120,256]{2,1,0:T(8,128)(2,1)} %param.13) | copy-start | bytes 7864324
  6.5 63.5 %reduce-scatter.7.cloned.1.call-start = ((), (), s32[]{:S(2)}) async-start(), calls=%async_computation.3 | async-start | bytes 655360
  8.3 2.1 %copy-start.1 = (bf16[1,5120,256]{2,1,0:T(8,128)(2,1)S(1)}, bf16[1,5120,256]{2,1,0:T(8,128)(2,1)}, u32[]{:S(2)}) copy-start(bf16[1,5120,256]{2,1,0:T(8,128)(2,1)} %param.14) | copy-start | bytes 7864324
  8.3 2.5 %copy-start.4 = (bf16[1,128,5120]{2,1,0:T(8,128)(2,1)S(1)}, bf16[1,128,5120]{2,1,0:T(8,128)(2,1)}, u32[]{:S(2)}) copy-start(bf16[1,128,5120]{2,1,0:T(8,128)(2,1)} %param.10) | copy-start | bytes 3932164
  11.3 12.6 %copy-start.8 = (s32[512]{0:T(512)S(1)}, s32[512]{0:T(512)}, u32[]{:S(2)}) copy-start(s32[512]{0:T(512)} %param.15) | copy-start | bytes 6148
  11.3 14.4 %copy-start.3 = (bf16[1,128,10,128]{3,1,2,0:T(8,128)(2,1)S(1)}, bf16[1,128,10,128]{3,1,2,0:T(8,128)(2,1)}, u32[]{:S(2)}) copy-start(bf16[1,128,10,128]{3,1,2,0:T(8,128)(2,1)} %param.11) | copy-start | bytes 983044
  11.3 14.4 %copy-start.5 = (bf16[1,128,10,128]{3,1,2,0:T(8,128)(2,1)S(1)}, bf16[1,128,10,128]{3,1,2,0:T(8,128)(2,1)}, u32[]{:S(2)}) copy-start(bf16[1,128,10,128]{3,1,2,0:T(8,128)(2,1)} %param.12) | copy-start | bytes 983044
  25.8 1.0 copy-start.6
  29.9 1.0 copy-start.6
  44.6 38.4 %reduce-scatter.5.cloned.1.call-start = ((), (), s32[]{:S(2)}) async-start(), calls=%async_computation.2 | async-start | bytes 1966080 | tf_op jit(solution)/shard_map/reduce_scatter | solution.py:106
  70.1 2.0 %copy-start.2 = (bf16[1,5120,256]{2,1,0:T(8,128)(2,1)S(1)}, bf16[1,5120,256]{2,1,0:T(8,128)(2,1)}, u32[]{:S(2)}) copy-start(bf16[1,5120,256]{2,1,0:T(8,128)(2,1)} %param.14) | copy-start | bytes 7864324
  70.1 2.0 %copy-start.7 = (bf16[128,512]{1,0:T(8,128)(2,1)S(1)}, bf16[128,512]{1,0:T(8,128)(2,1)}, u32[]{:S(2)}) copy-start(bf16[128,512]{1,0:T(8,128)(2,1)} %reduce-scatter.7.cloned.1.call-done) | copy-start | bytes 393220
  83.0 1.5 %collective-permute-start = (bf16[128,2560]{1,0:T(8,128)(2,1)}, bf16[128,2560]{1,0:T(8,128)(2,1)}, u32[]{:S(2)}, u32[]{:S(2)}) collective-permute-start(bf16[128,2560]{1,0:T(8,128)(2,1)} %reduce-scatter.5.cloned.1.call-done), channel_id=1, source_target_pairs={{24,16},{25,17},{26,18},{27,19},{28,20},{29,21},{30,22},{31,23}} | collective-permute-start | bytes 1966088 | tf_op jit(solution)/shard_map/ppermute | solution.py:13
  85.9 1.5 %collective-permute-start.1 = (bf16[128,2560]{1,0:T(8,128)(2,1)S(1)}, bf16[128,2560]{1,0:T(8,128)(2,1)}, u32[]{:S(2)}, u32[]{:S(2)}) collective-permute-start(bf16[128,2560]{1,0:T(8,128)(2,1)S(1)} %fusion.55), channel_id=1, source_target_pairs={{16,8},{17,9},{18,10},{19,11},{20,12},{21,13},{22,14},{23,15}} | collective-permute-start | bytes 1966088 | tf_op jit(solution)/shard_map/ppermute | solution.py:13
  90.1 50.0 %collective-permute-start.2 = (bf16[128,2560]{1,0:T(8,128)(2,1)}, bf16[128,2560]{1,0:T(8,128)(2,1)S(1)}, u32[]{:S(2)}, u32[]{:S(2)}) collective-permute-start(bf16[128,2560]{1,0:T(8,128)(2,1)} %fusion.66), channel_id=1, source_target_pairs={{8,0},{9,1},{10,2},{11,3},{12,4},{13,5},{14,6},{15,7}} | collective-permute-start | bytes 1966088 | tf_op jit(solution)/shard_map/ppermute | solution.py:13
Sparse Core Ops, SparseCore 0:
  44.7 25.3 reduce-scatter.6
  74.3 8.6 reduce-scatter.4
where the time goes:
time: 151 us; the launch traced here: 150 us
  waiting for transfers between devices  83 us (55%)
  matrix products  18 us (12%)
  between operations  13.5 us (9%)
  blocking collectives  11.7 us (8%)
  other arithmetic  11.1 us (7%)
  local copies, waits for them, and re-layouts  8.16 us (5%)
  starting transfers between devices  4.36 us (3%)
    ppermute x3, waiting for transfers between devices, suffix_chain(): lax.ppermute(total.astype(jnp.bfloat16), axis, [(src_dev, src_dev - 1)])  48.7 us
    unnamed x3, waiting for transfers between devices  25.5 us
    all_gather x1, blocking collectives, per_device(): lax.all_gather(jnp.concatenate((key_rows, value_rows), axis=1), 'ctx', ax...  11.7 us
    reduce_scatter x1, waiting for transfers between devices, per_device(): lax.psum_scatter(partial_sum.astype(jnp.bfloat16), 'head', scatter_dimens...  8.79 us
    ppermute x3, starting transfers between devices, suffix_chain(): lax.ppermute(total.astype(jnp.bfloat16), axis, [(src_dev, src_dev - 1)])  4.32 us
    dot_general x2, matrix products, per_group(): jnp.einsum('gts,tgd->sd', prob_group, grad_group, preferred_element_type=...  4.2 us
    unnamed x18, local copies, waits for them, and re-layouts  4.13 us
    convert_element_type x2, other arithmetic, suffix_chain(): total.astype(jnp.bfloat16)  4.12 us
  transfers between devices with their start and end apart: 5, of which 3 were waited for; matrix products, arithmetic and copies ran while one was open for 0% of the time, Pallas kernels for 0%

commit v1 on v0

--- a/solution.py
+++ b/solution.py
@@ -28,9 +28,23 @@
     value_rows = jnp.dot(tokens, w_value[0], preferred_element_type=jnp.float32).astype(
         jnp.bfloat16
     )
-    kv_all = lax.all_gather(
-        jnp.concatenate((key_rows, value_rows), axis=1), "ctx", axis=0, tiled=True
-    )
+    x = jnp.concatenate((key_rows, value_rows), axis=1)
+    size, mine, rows = (lax.axis_size("ctx"), lax.axis_index("ctx"), x.shape[0])
+    forward = [(i, (i + 1) % size) for i in range(size)]
+    backward = [(i, (i - 1) % size) for i in range(size)]
+    out = jnp.zeros((*x.shape[:0], size * rows, *x.shape[0 + 1 :]), x.dtype)
+    out = lax.dynamic_update_slice_in_dim(out, x, mine * rows, axis=0)
+    from_left = from_right = x
+    half = size // 2
+    for hop in range(1, half + 1):
+        from_left = lax.ppermute(from_left, "ctx", forward)
+        out = lax.dynamic_update_slice_in_dim(out, from_left, (mine - hop) % size * rows, axis=0)
+        if hop < size - half:
+            from_right = lax.ppermute(from_right, "ctx", backward)
+            out = lax.dynamic_update_slice_in_dim(
+                out, from_right, (mine + hop) % size * rows, axis=0
+            )
+    kv_all = out
     keys_all, values_all = (kv_all[:, : key_rows.shape[1]], kv_all[:, key_rows.shape[1] :])
     seq_rows = keys_all.shape[0]
     key_heads = keys_all.reshape(seq_rows, kv_local, head_dim)

time: 151 us -> 157 us (1.040)
  blocking collectives: 11.7 us -> 0 us
  waiting for transfers between devices: 83 us -> 89.3 us
  local copies, waits for them, and re-layouts: 8.16 us -> 13.9 us
  starting transfers between devices: 4.36 us -> 9.62 us
    all_gather x1 -> x0, blocking collectives: 11.7 us -> none  [per_device(): lax.all_gather(jnp.concatenate((key_rows, value_rows), axis=1), 'ctx', ax...]
    ppermute x0 -> x3, waiting for transfers between devices: none -> 5.39 us  [the longest x2 5.39 us: per_device(): from_left = lax.ppermute(from_left, 'ctx', forward)]
    ppermute x0 -> x3, starting transfers between devices: none -> 5.16 us  [the longest x2 4.14 us: per_device(): from_left = lax.ppermute(from_left, 'ctx', forward)]
    ppermute x0 -> x3, local copies, waits for them, and re-layouts: none -> 3.06 us  [the longest x2 2.04 us: per_device(): from_left = lax.ppermute(from_left, 'ctx', forward)]
    dynamic_update_slice x0 -> x4, local copies, waits for them, and re-layouts: none -> 2.75 us  [the longest x2 1.36 us: per_device(): lax.dynamic_update_slice_in_dim(out, from_left, (mine - hop) % size * row...]
    transpose x1 -> x0, local copies, waits for them, and re-layouts: 1.83 us -> none  [per_device(): jnp.moveaxis(value_heads, 1, 0)]
    slice x0 -> x1, local copies, waits for them, and re-layouts: none -> 1.75 us  [per_device(): kv_all[:, key_rows.shape[1]:]]
    unnamed x18 -> x19, local copies, waits for them, and re-layouts: 4.13 us -> 3.28 us
  transfers between devices with their start and end apart: 5 -> 8, of which waited for: 3 -> 5; matrix products, arithmetic and copies ran while one was open for 0% -> 3% of each run, Pallas kernels for 0% -> 0%
where the time goes in v1:
time: 157 us; the launch traced here: 156 us
  waiting for transfers between devices  89.3 us (57%)
  matrix products  18 us (11%)
  local copies, waits for them, and re-layouts  13.9 us (9%)
  between operations  13.5 us (9%)
  other arithmetic  11.7 us (7%)
  starting transfers between devices  9.62 us (6%)
    ppermute x3, waiting for transfers between devices, suffix_chain(): lax.ppermute(total.astype(jnp.bfloat16), axis, [(src_dev, src_dev - 1)])  49.1 us
    unnamed x3, waiting for transfers between devices  26.1 us
    reduce_scatter x1, waiting for transfers between devices, per_device(): lax.psum_scatter(partial_sum.astype(jnp.bfloat16), 'head', scatter_dimens...  8.79 us
    ppermute x2, waiting for transfers between devices, per_device(): from_left = lax.ppermute(from_left, 'ctx', forward)  5.39 us
    convert_element_type x2, other arithmetic, suffix_chain(): total.astype(jnp.bfloat16)  4.76 us
    ppermute x3, starting transfers between devices, suffix_chain(): lax.ppermute(total.astype(jnp.bfloat16), axis, [(src_dev, src_dev - 1)])  4.42 us
    dot_general x2, matrix products, per_group(): jnp.einsum('gts,tgd->sd', prob_group, grad_group, preferred_element_type=...  4.19 us
    ppermute x2, starting transfers between devices, per_device(): from_left = lax.ppermute(from_left, 'ctx', forward)  4.14 us
  transfers between devices with their start and end apart: 8, of which 5 were waited for; matrix products, arithmetic and copies ran while one was open for 3% of the time, Pallas kernels for 0%

profile of v1, /device:TPU:0, one launch (start us, length us, event | category | flops | bytes accessed | tf_op | source)
XLA Modules:
  0.0 156.3 jit_solution(7984608621218963425)
XLA Ops:
  6.5 1.7 %copy-done = bf16[1,5120,256]{2,1,0:T(8,128)(2,1)S(1)} copy-done((bf16[1,5120,256]{2,1,0:T(8,128)(2,1)S(1)}, bf16[1,5120,256]{2,1,0:T(8,128)(2,1)}, u32[]{:S(2)}) %copy-start) | copy-done | bytes 2621464
  8.3 2.0 %fusion.56 = bf16[128,256]{1,0:T(8,128)(2,1)S(1)} fusion(bf16[1,5120,256]{2,1,0:T(8,128)(2,1)S(1)} %copy-done, bf16[1,128,5120]{2,1,0:T(8,128)(2,1)} %param.10), kind=kOutput, calls=%fused_computation.71 | convolution fusion | flops 335577088 | bytes 3997696 | tf_op jit(solution)/shard_map/dot_general | solution.py:27
  10.4 0.4 copy-done.5
  10.8 0.5 fusion.61
  11.3 3.0 %collective-permute-start = (bf16[128,512]{1,0:T(8,128)(2,1)S(1)}, bf16[128,512]{1,0:T(8,128)(2,1)}, u32[]{:S(2)}, u32[]{:S(2)}) collective-permute-start(bf16[128,512]{1,0:T(8,128)(2,1)S(1)} %pad_maximum_fusion.1), channel_id=1, source_target_pairs={{0,2},{2,4},{4,6},{6,0},{1,3},{3,5},{5,7},{7,1},{8,10},{10,12},{12... | collective-permute-start | bytes 393224 | tf_op jit(solution)/shard_map/ppermute | solution.py:40
  14.3 1.0 collective-permute-start.1
  15.5 0.8 broadcast_in_dim.40
  16.3 0.7 constant_dynamic-update-slice_fusion.4
  17.1 2.7 %collective-permute-done = bf16[128,512]{1,0:T(8,128)(2,1)} collective-permute-done((bf16[128,512]{1,0:T(8,128)(2,1)S(1)}, bf16[128,512]{1,0:T(8,128)(2,1)}, u32[]{:S(2)}, u32[]{:S(2)}) %collective-permute-start) | collective-permute-done | bytes 131104 | tf_op jit(solution)/shard_map/ppermute | solution.py:40
  19.7 1.0 copy.25
  20.8 1.1 collective-permute-start.2
  21.9 0.7 constant_dynamic-update-slice_fusion.3
  22.6 1.0 copy.26
  23.6 0.7 constant_dynamic-update-slice_fusion.2
  24.3 2.7 %collective-permute-done.2 = bf16[128,512]{1,0:T(8,128)(2,1)} collective-permute-done((bf16[128,512]{1,0:T(8,128)(2,1)}, bf16[128,512]{1,0:T(8,128)(2,1)}, u32[]{:S(2)}, u32[]{:S(2)}) %collective-permute-start.2) | collective-permute-done | bytes 131104 | tf_op jit(solution)/shard_map/ppermute | solution.py:40
  27.0 1.0 copy.27
  28.0 0.7 constant_dynamic-update-slice_fusion.1
  28.7 1.8 %fusion.70 = (bf16[512,256]{0,1:T(8,128)(2,1)}, bf16[512,256]{0,1:T(8,128)(2,1)S(1)}) fusion(bf16[512,512]{0,1:T(8,128)(2,1)} %constant_dynamic-update-slice_fusion.1), kind=kLoop, calls=%fused_computation.85 | loop fusion | bytes 1048576 | tf_op jit(solution)/shard_map/slice | solution.py:48
  30.5 8.1 %while.26 = (s32[]{:T(128)}, bf16[2,5,128,512]{2,3,1,0:T(8,128)(2,1)}, bf16[2,5,128,512]{2,3,1,0:T(8,128)(2,1)}, bf16[2,512,128]{1,2,0:T(8,128)(2,1)S(1)}, bf16[...) while((s32[]{:T(128)}, ...), condition=%wide.region_4.5_spmd.clone, body=%wide.region_0.4_spmd.clone.sunk | while | flops 257735424 | bytes 10228865 | solution.py:88
  30.6 0.4 fusion.96
  31.6 0.6 fusion.97
  32.1 1.3 fusion.98
  33.5 1.1 bitcast_dynamic-update-slice_fusion.2
  34.7 0.4 fusion.96
  35.3 0.3 copy-done.7
  35.6 0.6 fusion.97
  36.2 1.3 fusion.98
  37.5 1.1 bitcast_dynamic-update-slice_fusion.2
  38.6 8.6 %while.25 = (s32[]{:T(128)}, bf16[2,512,128]{1,2,0:T(8,128)(2,1)}, bf16[2,512,128]{1,2,0:T(8,128)(2,1)}, bf16[2,5,128,512]{2,3,1,0:T(8,128)(2,1)}, bf16[2,128,5,...) while((s32[]{:T(128)}, bf16[2,512,128]{1,2,0:T(8,128)(2,1)}, ...), condition=%wide.region_6.7_spmd, body=%wide.region_5.6_spmd.sunk | while | flops 167903232 | bytes 2559061 | solution.py:104
  38.6 1.4 fusion.89
  40.1 0.7 constant_dynamic-update-slice_fusion.6
  40.8 2.1 %fusion.90 = bf16[2,512,128]{1,2,0:T(8,128)(2,1)} fusion(bf16[2,512,128]{1,2,0:T(8,128)(2,1)} %get-tuple-element.308, s32[]{:T(128)} %get-tuple-element.306, bf16[2,5,128,512]{2,3,1,0:T(8,128)(2,1)} %get-tuple-element.319, bf16[2,128,5,128]{3,1,2,0:T(8,128)(2,1)S(1)} %get-tuple-element.320), kind=kOutput, calls=%fused_computation.2.clone.1 | convolution fusion | flops 83886080 | bytes 1082880 | tf_op jit(solution)/shard_map/while/body/eval_jaxpr/gts,tgd->sd/dot_general | solution.py:95
  42.9 1.4 fusion.89
  44.4 0.7 constant_dynamic-update-slice_fusion.6
  45.1 2.1 %fusion.90 = bf16[2,512,128]{1,2,0:T(8,128)(2,1)} fusion(bf16[2,512,128]{1,2,0:T(8,128)(2,1)} %get-tuple-element.308, s32[]{:T(128)} %get-tuple-element.306, bf16[2,5,128,512]{2,3,1,0:T(8,128)(2,1)} %get-tuple-element.319, bf16[2,128,5,128]{3,1,2,0:T(8,128)(2,1)S(1)} %get-tuple-element.320), kind=kOutput, calls=%fused_computation.2.clone.1 | convolution fusion | flops 83886080 | bytes 1082880 | tf_op jit(solution)/shard_map/while/body/eval_jaxpr/gts,tgd->sd/dot_general | solution.py:95
  47.2 1.1 pad_maximum_fusion
  48.3 1.0 copy.36
  49.3 26.0 %reduce-scatter.7.cloned.1.call-done = bf16[128,512]{1,0:T(8,128)(2,1)} async-done(((bf16[512,512]{1,0:T(8,128)(2,1)}), bf16[128,512]{1,0:T(8,128)(2,1)}) %reduce-scatter.7.cloned.1.call-update) | async-done | bytes 131088
  75.4 2.0 %fusion.46 = f32[128,5120]{1,0:T(8,128)S(1)} fusion(bf16[1,5120,256]{2,1,0:T(8,128)(2,1)S(1)} %copy-done, bf16[128,512]{1,0:T(8,128)(2,1)} %reduce-scatter.7.cloned.1.call-done), kind=kOutput, calls=%fused_computation.57 | convolution fusion | flops 335544320 | bytes 5308416 | tf_op jit(solution)/shard_map/dot_general | solution.py:116
  77.4 2.0 %fusion.42 = bf16[128,5120]{1,0:T(8,128)(2,1)} fusion(f32[128,5120]{1,0:T(8,128)S(1)} %fusion.46, bf16[1,5120,256]{2,1,0:T(8,128)(2,1)S(1)} %copy-done.2, bf16[128,512]{1,0:T(8,128)(2,1)S(1)} %copy-done.8), kind=kOutput, calls=%fused_computation.53 | convolution fusion | flops 336855040 | bytes 6619136 | tf_op jit(solution)/shard_map/dot_general | solution.py:117
  79.4 8.8 %reduce-scatter.5.cloned.1.call-done = bf16[128,2560]{1,0:T(8,128)(2,1)} async-done(((bf16[128,5120]{1,0:T(8,128)(2,1)}), bf16[128,2560]{1,0:T(8,128)(2,1)}) %reduce-scatter.5.cloned.1.call-update) | async-done | bytes 655376 | tf_op jit(solution)/shard_map/reduce_scatter | solution.py:120
  88.2 1.6 %collective-permute-start.3 = (bf16[128,2560]{1,0:T(8,128)(2,1)}, bf16[128,2560]{1,0:T(8,128)(2,1)}, u32[]{:S(2)}, u32[]{:S(2)}) collective-permute-start(bf16[128,2560]{1,0:T(8,128)(2,1)} %reduce-scatter.5.cloned.1.call-done), channel_id=1, source_target_pairs={{24,16},{25,17},{26,18},{27,19},{28,20},{29,21},{30,22},{31,23}} | collective-permute-start | bytes 1966088 | tf_op jit(solution)/shard_map/ppermute | solution.py:13
  89.9 2.3 %fusion.55 = bf16[128,2560]{1,0:T(8,128)(2,1)} fusion(bf16[128,2560]{1,0:T(8,128)(2,1)} %collective-permute-done.3, bf16[128,2560]{1,0:T(8,128)(2,1)} %reduce-scatter.5.cloned.1.call-done, pred[]{:T(512)S(6)} %eq.34), kind=kLoop, calls=%fused_computation.70 | loop fusion | flops 1638400 | bytes 1966081 | tf_op jit(solution)/shard_map/convert_element_type | solution.py:13
  92.2 1.5 collective-permute-start.4
  93.7 2.4 %fusion.66 = bf16[128,2560]{1,0:T(8,128)(2,1)} fusion(bf16[128,2560]{1,0:T(8,128)(2,1)} %collective-permute-done.3, bf16[128,2560]{1,0:T(8,128)(2,1)} %collective-permute-done.4, bf16[128,2560]{1,0:T(8,128)(2,1)S(1)} %copy-done.4, pred[]{:T(512)S(6)} %eq.34, pred[]{:T(512)S(6)} %eq.33), kind=kLoop, calls=%fused_computation.73 | loop fusion | flops 2621440 | bytes 2621442 | tf_op jit(solution)/shard_map/convert_element_type | solution.py:13
  96.1 1.3 collective-permute-start.5
  97.4 49.1 %collective-permute-done.5 = bf16[128,2560]{1,0:T(8,128)(2,1)} collective-permute-done((bf16[128,2560]{1,0:T(8,128)(2,1)}, bf16[128,2560]{1,0:T(8,128)(2,1)}, u32[]{:S(2)}, u32[]{:S(2)}) %collective-permute-start.5) | collective-permute-done | bytes 655392 | tf_op jit(solution)/shard_map/ppermute | solution.py:13
  146.5 3.0 %fusion.52 = f32[1,128,2560]{2,1,0:T(8,128)} fusion(bf16[128,2560]{1,0:T(8,128)(2,1)S(1)} %copy-done.4, bf16[128,2560]{1,0:T(8,128)(2,1)} %collective-permute-done.5, bf16[128,2560]{1,0:T(8,128)(2,1)} %collective-permute-done.3, bf16[128,2560]{1,0:T(8,128)(2,1)} %collective-permute-done.4, pred[]{:T(512)S(6)} %eq.34, pred[]{:T(512)S(6)} %eq.33, pred[]{:T(512)S(6)} %eq.29), kind=kLoop, calls=%fused_computation.67 | loop fusion | flops 3276800 | bytes 3932163 | tf_op jit(solution)/shard_map/broadcast_in_dim | solution.py:124
  (42 shorter events, 1.7 us)
Async XLA Ops:
  6.5 1.7 %copy-start = (bf16[1,5120,256]{2,1,0:T(8,128)(2,1)S(1)}, bf16[1,5120,256]{2,1,0:T(8,128)(2,1)}, u32[]{:S(2)}) copy-start(bf16[1,5120,256]{2,1,0:T(8,128)(2,1)} %param.13) | copy-start | bytes 7864324
  6.5 68.8 %reduce-scatter.7.cloned.1.call-start = ((), (), s32[]{:S(2)}) async-start(), calls=%async_computation.3 | async-start | bytes 655360
  8.3 2.1 %copy-start.1 = (bf16[1,5120,256]{2,1,0:T(8,128)(2,1)S(1)}, bf16[1,5120,256]{2,1,0:T(8,128)(2,1)}, u32[]{:S(2)}) copy-start(bf16[1,5120,256]{2,1,0:T(8,128)(2,1)} %param.14) | copy-start | bytes 7864324
  8.3 2.5 %copy-start.5 = (bf16[1,128,5120]{2,1,0:T(8,128)(2,1)S(1)}, bf16[1,128,5120]{2,1,0:T(8,128)(2,1)}, u32[]{:S(2)}) copy-start(bf16[1,128,5120]{2,1,0:T(8,128)(2,1)} %param.10) | copy-start | bytes 3932164
  10.8 4.7 %copy-start.9 = (s32[512]{0:T(512)S(1)}, s32[512]{0:T(512)}, u32[]{:S(2)}) copy-start(s32[512]{0:T(512)} %param.15) | copy-start | bytes 6148
  11.3 8.4 %collective-permute-start = (bf16[128,512]{1,0:T(8,128)(2,1)S(1)}, bf16[128,512]{1,0:T(8,128)(2,1)}, u32[]{:S(2)}, u32[]{:S(2)}) collective-permute-start(bf16[128,512]{1,0:T(8,128)(2,1)S(1)} %pad_maximum_fusion.1), channel_id=1, source_target_pairs={{0,2},{2,4},{4,6},{6,0},{1,3},{3,5},{5,7},{7,1},{8,10},{10,12},{12... | collective-permute-start | bytes 393224 | tf_op jit(solution)/shard_map/ppermute | solution.py:40
  14.3 8.2 %collective-permute-start.1 = (bf16[128,512]{1,0:T(8,128)(2,1)S(1)}, bf16[128,512]{1,0:T(8,128)(2,1)}, u32[]{:S(2)}, u32[]{:S(2)}) collective-permute-start(bf16[128,512]{1,0:T(8,128)(2,1)S(1)} %pad_maximum_fusion.1), channel_id=1, source_target_pairs={{0,6},{2,0},{4,2},{6,4},{1,7},{3,1},{5,3},{7,5},{8,14},{10,8},{12,... | collective-permute-start | bytes 393224 | tf_op jit(solution)/shard_map/ppermute | solution.py:43
  17.0 13.4 %copy-start.3 = (bf16[1,128,10,128]{3,1,2,0:T(8,128)(2,1)S(1)}, bf16[1,128,10,128]{3,1,2,0:T(8,128)(2,1)}, u32[]{:S(2)}) copy-start(bf16[1,128,10,128]{3,1,2,0:T(8,128)(2,1)} %param.11) | copy-start | bytes 983044
  17.1 13.4 %copy-start.6 = (bf16[1,128,10,128]{3,1,2,0:T(8,128)(2,1)S(1)}, bf16[1,128,10,128]{3,1,2,0:T(8,128)(2,1)}, u32[]{:S(2)}) copy-start(bf16[1,128,10,128]{3,1,2,0:T(8,128)(2,1)} %param.12) | copy-start | bytes 983044
  20.8 6.2 %collective-permute-start.2 = (bf16[128,512]{1,0:T(8,128)(2,1)}, bf16[128,512]{1,0:T(8,128)(2,1)}, u32[]{:S(2)}, u32[]{:S(2)}) collective-permute-start(bf16[128,512]{1,0:T(8,128)(2,1)} %collective-permute-done), channel_id=1, source_target_pairs={{0,2},{2,4},{4,6},{6,0},{1,3},{3,5},{5,7},{7,1},{8,10},{10,12},{12... | collective-permute-start | bytes 393224 | tf_op jit(solution)/shard_map/ppermute | solution.py:40
  30.6 1.0 copy-start.7
  34.7 1.0 copy-start.7
  49.3 38.9 %reduce-scatter.5.cloned.1.call-start = ((), (), s32[]{:S(2)}) async-start(), calls=%async_computation.2 | async-start | bytes 1966080 | tf_op jit(solution)/shard_map/reduce_scatter | solution.py:120
  75.4 2.0 %copy-start.2 = (bf16[1,5120,256]{2,1,0:T(8,128)(2,1)S(1)}, bf16[1,5120,256]{2,1,0:T(8,128)(2,1)}, u32[]{:S(2)}) copy-start(bf16[1,5120,256]{2,1,0:T(8,128)(2,1)} %param.14) | copy-start | bytes 7864324
  75.4 2.0 %copy-start.8 = (bf16[128,512]{1,0:T(8,128)(2,1)S(1)}, bf16[128,512]{1,0:T(8,128)(2,1)}, u32[]{:S(2)}) copy-start(bf16[128,512]{1,0:T(8,128)(2,1)} %reduce-scatter.7.cloned.1.call-done) | copy-start | bytes 393220
  88.2 5.5 %copy-start.4 = (bf16[128,2560]{1,0:T(8,128)(2,1)S(1)}, bf16[128,2560]{1,0:T(8,128)(2,1)}, u32[]{:S(2)}) copy-start(bf16[128,2560]{1,0:T(8,128)(2,1)} %reduce-scatter.5.cloned.1.call-done) | copy-start | bytes 1966084
  88.2 1.6 %collective-permute-start.3 = (bf16[128,2560]{1,0:T(8,128)(2,1)}, bf16[128,2560]{1,0:T(8,128)(2,1)}, u32[]{:S(2)}, u32[]{:S(2)}) collective-permute-start(bf16[128,2560]{1,0:T(8,128)(2,1)} %reduce-scatter.5.cloned.1.call-done), channel_id=1, source_target_pairs={{24,16},{25,17},{26,18},{27,19},{28,20},{29,21},{30,22},{31,23}} | collective-permute-start | bytes 1966088 | tf_op jit(solution)/shard_map/ppermute | solution.py:13
  92.2 1.5 collective-permute-start.4
  96.1 50.4 %collective-permute-start.5 = (bf16[128,2560]{1,0:T(8,128)(2,1)}, bf16[128,2560]{1,0:T(8,128)(2,1)}, u32[]{:S(2)}, u32[]{:S(2)}) collective-permute-start(bf16[128,2560]{1,0:T(8,128)(2,1)} %fusion.66), channel_id=1, source_target_pairs={{8,0},{9,1},{10,2},{11,3},{12,4},{13,5},{14,6},{15,7}} | collective-permute-start | bytes 1966088 | tf_op jit(solution)/shard_map/ppermute | solution.py:13
Sparse Core Ops, SparseCore 0:
  49.4 25.9 reduce-scatter.6
  79.6 8.6 reduce-scatter.4
